TPU v7x, 128 devices: a whole 4x4x4 slice. The times are simulated.
128 devices in a mesh: req: 16 (over y, x), kv: 8 (over z, core).
Axes of the slice: x: 4, y: 4, z: 4, core: 2. Of those that a mesh axis runs over, the one named last changes fastest.
Arguments:
- hidden: bfloat16 [1024, 1536], P('req', 'kv'), may hold values from -6 to 6
- perm: int32 [1024], replicated, may hold values from 0 to 1023, as said below
- seq_lens: int32 [1024], P('req'), may hold values from 1 to 4096, as said below
- page_table: int32 [1024, 32], P('req'), may hold values from 0 to 319, as said below
- kv_cache: bfloat16 [5120, 8, 128, 128], P('req', 'kv'), may hold values from -52 to 52
- attn_gain: float32 [1536], replicated, may hold values from 0.1 to 1.9
- qkv_weight: bfloat16 [8, 1536, 320], P('kv'), may hold values from -0.15625 to 0.15625
- out_weight: bfloat16 [8, 192, 1536], P('kv'), may hold values from -1 to 1
- ffn_gain: float32 [1536], replicated, may hold values from 0.1 to 1.9
- router: bfloat16 [1536, 16], replicated, may hold values from -0.15625 to 0.15625
- routes: int32 [1024, 2], P(('req', 'kv')), may hold values from 0 to 15, all different within a row; in each aligned block of 8 rows (0 to 7, 8 to 15, ...) at most 2 rows name the same one
- gate_up: bfloat16 [16, 1536, 2048], P('req'), may hold values from -0.15625 to 0.15625
- down: bfloat16 [16, 1024, 1536], P('req'), may hold values from -0.1875 to 0.1875
Outputs:
- mixed: bfloat16 [1024, 1536], P(('req', 'kv'))
Inputs may be any that keep to these rules, and one draw needn't show every extreme that they name: A permutation of the 1024 requests: slot s holds request perm[s]. The 64 slots of each index of req hold exactly 4 requests from each block of 64 consecutive requests. `seq_lens`: the length 4096 is reached on every index of req. `page_table`: entries 0 to (seq_lens[s] + 127) // 128 - 1 of row s are used; no page of one index of req is used by two of its slots; later entries name arbitrary pages.
All inputs are finite; a program needn't handle non-finite values.
Results may differ from a plain program's by a relative error of at most 0.017.
Values may be sent and summed in bfloat16 or wider, within the bound.
No kernel may reach another device: no remote copies, remote signals or barrier semaphores. Data moves between devices by JAX's collectives and lax.ppermute only.
A program may use at most 128 MiB of HBM per device.

v0:
```python
import jax
import jax.numpy as jnp
from jax import lax
from jax.sharding import PartitionSpec as P

REQ_DEV = 64
NEG_FILL = -1e30
EPS_NORM = 1e-05


def rms_norm(values, gain_vec):
    values = values.astype(jnp.float32)
    factor = lax.rsqrt(jnp.mean(values * values, axis=-1, keepdims=True) + EPS_NORM)
    return (values * factor * gain_vec).astype(jnp.bfloat16)


def attend(normed, seq_lens, page_table, kv_cache, qkv_weight):
    pool_pages, local_heads, twice_hd, page_len = kv_cache.shape
    head_dim = twice_hd // 2
    slot_count = normed.shape[0]
    groups = qkv_weight.shape[2] // head_dim - 2
    max_pages = page_table.shape[1]
    projected = jnp.einsum("sd,hdc->shc", normed, qkv_weight, preferred_element_type=jnp.float32)
    queries = (
        projected[:, :, : groups * head_dim]
        .reshape(slot_count, local_heads, groups, head_dim)
        .astype(jnp.bfloat16)
    )
    key_new = projected[:, :, groups * head_dim : (groups + 1) * head_dim].astype(jnp.bfloat16)
    value_new = projected[:, :, (groups + 1) * head_dim :].astype(jnp.bfloat16)
    page_need = (seq_lens + page_len - 1) // page_len
    page_ids = jnp.arange(max_pages, dtype=jnp.int32)
    in_use = page_ids[None, :] < page_need[:, None]
    pool_ids = jnp.arange(pool_pages, dtype=jnp.int32)
    match = (page_table[:, :, None] == pool_ids[None, None, :]) & in_use[:, :, None]
    belongs = jnp.any(match, axis=1)
    page_order = jnp.sum(jnp.where(match, page_ids[None, :, None], 0), axis=(0, 1))
    owner_len = jnp.sum(jnp.where(belongs, seq_lens[:, None], 0), axis=0)
    position = page_order[:, None] * page_len + jnp.arange(page_len, dtype=jnp.int32)[None, :]
    live = position < owner_len[:, None]
    scale_factor = head_dim ** (-0.5)
    page_queries = (
        jnp.dot(
            belongs.T.astype(jnp.bfloat16),
            queries.reshape(slot_count, -1),
            preferred_element_type=jnp.float32,
        )
        .astype(jnp.bfloat16)
        .reshape(pool_pages, local_heads, groups, head_dim)
    )
    scores = (
        jnp.einsum(
            "pkgd,pkdt->pkgt",
            page_queries,
            kv_cache[:, :, :head_dim, :],
            preferred_element_type=jnp.float32,
        )
        * scale_factor
    )
    scores = jnp.where(live[:, None, None, :], scores, NEG_FILL)
    score_new = (
        jnp.einsum("skgd,skd->skg", queries, key_new, preferred_element_type=jnp.float32)
        * scale_factor
    )
    page_peak = jnp.max(scores, axis=3)
    slot_peak = jnp.max(jnp.where(belongs[:, :, None, None], page_peak[None], NEG_FILL), axis=1)
    slot_peak = jnp.maximum(slot_peak, score_new)
    page_peak_of_owner = jnp.max(
        jnp.where(belongs[:, :, None, None], slot_peak[:, None], NEG_FILL), axis=0
    )
    weights = jnp.where(
        live[:, None, None, :], jnp.exp(scores - page_peak_of_owner[..., None]), 0.0
    )
    page_total = jnp.sum(weights, axis=3)
    page_value = jnp.einsum(
        "pkgt,pkdt->pkgd",
        weights.astype(jnp.bfloat16),
        kv_cache[:, :, head_dim:, :],
        preferred_element_type=jnp.float32,
    )
    belongs_f = belongs.astype(jnp.float32)
    total_sum = jnp.dot(
        belongs_f, page_total.reshape(pool_pages, -1), precision=lax.Precision.HIGHEST
    ).reshape(slot_count, local_heads, groups)
    value_sum = jnp.dot(
        belongs_f, page_value.reshape(pool_pages, -1), precision=lax.Precision.HIGHEST
    ).reshape(slot_count, local_heads, groups, head_dim)
    weight_new = jnp.exp(score_new - slot_peak)
    total_sum = total_sum + weight_new
    rounded_new = lax.optimization_barrier(weight_new.astype(jnp.bfloat16)).astype(jnp.float32)
    value_sum = value_sum + rounded_new[..., None] * value_new.astype(jnp.float32)[:, :, None, :]
    return (value_sum / total_sum[..., None]).astype(jnp.bfloat16).reshape(slot_count, -1)


def expert_apply(piece, gate_up, down):
    n_source, slot_num, local_experts, width = piece.shape
    rows_in = piece.transpose(2, 0, 1, 3).reshape(local_experts, n_source * slot_num, width)
    projected_up = jnp.einsum("erd,edf->erf", rows_in, gate_up, preferred_element_type=jnp.float32)
    hidden_units = gate_up.shape[2] // 2
    acts = (
        jax.nn.silu(projected_up[..., :hidden_units]) * projected_up[..., hidden_units:]
    ).astype(jnp.bfloat16)
    result = jnp.einsum("erf,efd->erd", acts, down, preferred_element_type=jnp.float32).astype(
        jnp.bfloat16
    )
    return result.reshape(local_experts, n_source, slot_num, width).transpose(1, 2, 0, 3)


def shards(
    hidden,
    perm,
    seq_lens,
    page_table,
    kv_cache,
    attn_gain,
    qkv_weight,
    out_weight,
    ffn_gain,
    router,
    routes,
    gate_up,
    down,
):
    req_index = lax.axis_index("req")
    kv_index = lax.axis_index("kv")
    every_row = lax.all_gather(hidden, "req", axis=0, tiled=True)
    my_perm = lax.dynamic_slice_in_dim(perm, req_index * REQ_DEV, REQ_DEV)
    pick = (my_perm[:, None] == jnp.arange(every_row.shape[0], dtype=jnp.int32)[None, :]).astype(
        every_row.dtype
    )
    picked_rows = jnp.dot(pick, every_row, preferred_element_type=jnp.float32).astype(
        every_row.dtype
    )
    tokens = lax.all_gather(picked_rows, "kv", axis=1, tiled=True)
    normed = rms_norm(tokens, attn_gain)
    head_out = attend(normed, seq_lens, page_table, kv_cache, qkv_weight)
    sub_rows = routes.shape[0]
    width = tokens.shape[1]
    out_flat = out_weight.reshape(-1, out_weight.shape[2])
    attn_rows = lax.psum_scatter(
        jnp.dot(head_out, out_flat, preferred_element_type=jnp.float32).astype(jnp.bfloat16),
        "kv",
        scatter_dimension=0,
        tiled=True,
    ).astype(jnp.float32)
    own_tokens = lax.dynamic_slice_in_dim(tokens, kv_index * sub_rows, sub_rows, 0)
    residual = (own_tokens.astype(jnp.float32) + attn_rows).astype(jnp.bfloat16)
    normed_ffn = rms_norm(residual, ffn_gain)
    logits = jnp.dot(normed_ffn, router, preferred_element_type=jnp.float32)
    chosen = jnp.take_along_axis(logits, routes, axis=1)
    sigmoid_vals = jax.nn.sigmoid(chosen)
    gates = sigmoid_vals / jnp.sum(sigmoid_vals, axis=1, keepdims=True)
    experts_all = router.shape[1]
    n_req = lax.axis_size("req")
    local_experts = gate_up.shape[0]
    capacity = max(2, 2 * sub_rows // experts_all + 1)
    flat_routes = routes.reshape(-1)
    onehot_int = (flat_routes[:, None] == jnp.arange(experts_all, dtype=jnp.int32)[None, :]).astype(
        jnp.int32
    )
    earlier = jnp.cumsum(onehot_int, axis=0) - onehot_int
    rank_in = jnp.sum(earlier * onehot_int, axis=1)
    place_at = (
        flat_routes // local_experts * capacity * local_experts
        + rank_in * local_experts
        + flat_routes % local_experts
    )
    placement_plan = (
        place_at[:, None] == jnp.arange(experts_all * capacity, dtype=jnp.int32)[None, :]
    ).astype(jnp.bfloat16)
    paired_rows = jnp.repeat(normed_ffn, 2, axis=0)
    outgoing = jnp.einsum(
        "qe,qd->ed", placement_plan, paired_rows, preferred_element_type=jnp.float32
    )
    outgoing = outgoing.astype(jnp.bfloat16).reshape(n_req, capacity, local_experts, width)
    arrived = lax.all_to_all(outgoing, "req", split_axis=0, concat_axis=0, tiled=True)
    returned = lax.all_to_all(
        expert_apply(arrived, gate_up, down), "req", split_axis=0, concat_axis=0, tiled=True
    )
    back_rows = returned.reshape(experts_all * capacity, width)
    paired_output = jnp.dot(placement_plan, back_rows, preferred_element_type=jnp.float32).reshape(
        sub_rows, 2, width
    )
    mixed = residual.astype(jnp.float32) + jnp.sum(gates[:, :, None] * paired_output, axis=1)
    return mixed.astype(jnp.bfloat16)


def solution(mesh):
    in_specs = (
        P("req", "kv"),
        P(),
        P("req"),
        P("req", None),
        P("req", "kv", None, None),
        P(),
        P("kv", None, None),
        P("kv", None, None),
        P(),
        P(),
        P(("req", "kv"), None),
        P("req", None, None),
        P("req", None, None),
    )
    out_specs = P(("req", "kv"), None)
    return jax.shard_map(shards, mesh=mesh, in_specs=in_specs, out_specs=out_specs, check_vma=False)
```

profile of v0, /device:TPU:0, one launch (start us, length us, event | category | flops | bytes accessed | tf_op | source)
XLA Modules:
  0.0 153.1 jit_solution(15035684609703527632)
XLA Ops:
  6.5 0.9 copy.88
  7.5 0.7 and_select_fusion
  8.2 0.9 fusion.7
  9.1 0.8 select_reduce_fusion
  10.0 26.8 %all_gather.6 = bf16[1024,192]{1,0:T(8,128)(2,1)} all-gather(bf16[64,192]{1,0:T(8,128)(2,1)} %param.13), channel_id=1, replica_groups=mesh['req'=16,'kv'=8] {'req'}, dimensions={0}, use_global_device_ids=true | all-gather | bytes 417792 | tf_op jit(solution)/shard_map/all_gather | solution.py:126
  36.8 0.8 dynamic_slice.6
  37.6 1.3 fusion.19
  38.9 14.0 %all-gather = bf16[8,192,64]{1,2,0:T(8,128)(2,1)S(1)} all-gather(bf16[1,192,64]{1,2,0:T(8,128)(2,1)S(1)} %fusion.19), channel_id=1, replica_groups=mesh['req'=16,'kv'=8] {'kv'}, dimensions={0}, use_global_device_ids=true | all-gather | bytes 221184 | tf_op jit(solution)/shard_map/all_gather | solution.py:134
  52.9 0.8 copy.87
  53.7 1.2 reshape.301
  55.1 0.8 select_reduce_fusion.3
  55.8 1.6 %convolution_bitcast_fusion = bf16[64,1,320]{2,0,1:T(8,128)(2,1)S(1)} fusion(bf16[1,1536,320]{1,2,0:T(8,128)(2,1)} %param.19, bf16[1536,64]{0,1:T(8,128)(2,1)S(1)} %reshape.301, f32[1536]{0:T(1024)} %param.18, f32[64]{0:T(128)S(1)} %add_rsqrt_fusion.1), kind=kOutput, calls=%fused_computation.20 | convolution fusion | flops 63307776 | bytes 1227008 | tf_op jit(solution)/shard_map/sd,hdc->shc/dot_general | solution.py:23
  57.7 0.7 fusion.47
  58.4 0.9 copy.90
  59.5 5.6 %fusion.57 = (f32[320,3]{1,0:T(8,128)}, f32[320,3,128]{2,1,0:T(4,128)}) fusion(bf16[320,3,64]{2,1,0:T(4,128)(2,1)} %copy.90, bf16[320,1,128,128]{3,2,0,1:T(8,128)(2,1)} %bitcast.113, pred[320,128]{1,0:T(8,128)(4,1)S(1)} %add_compare_fusion), kind=kOutput, calls=%fused_computation.102 | convolution fusion | flops 16096320 | bytes 6106880 | tf_op jit(solution)/shard_map/pkgd,pkdt->pkgt/dot_general | solution.py:52
  65.2 1.0 copy.91
  66.9 1.9 %fusion.22 = f32[320,3]{1,0:T(8,128)S(1)} fusion(f32[320,3,128]{2,1,0:T(4,128)} %get-tuple-element.14, f32[320,3]{1,0:T(8,128)S(1)} %copy.93, pred[320,128]{1,0:T(8,128)(4,1)} %copy-done.2), kind=kLoop, calls=%fused_computation.34 | loop fusion | flops 367680 | bytes 540160 | tf_op jit(solution)/shard_map/reduce_sum | solution.py:74
  68.8 6.5 %fusion.2 = f32[320,3,64]{2,1,0:T(4,128)} fusion(bf16[320,1,128,128]{3,2,0,1:T(8,128)(2,1)} %bitcast.114, f32[320,3,128]{2,1,0:T(4,128)} %get-tuple-element.14, f32[320,3]{1,0:T(8,128)S(1)} %copy.93, pred[320,128]{1,0:T(8,128)(4,1)} %copy-done.2), kind=kOutput, calls=%fused_computation.4 | convolution fusion | flops 16097280 | bytes 6188800 | tf_op jit(solution)/shard_map/pkgt,pkdt->pkgd/dot_general | solution.py:75
  75.5 2.1 %copy.95 = f32[320,3,64]{0,2,1:T(8,128)} copy(f32[320,3,64]{2,1,0:T(4,128)} %fusion.2) | data formatting | bytes 491520 | tf_op jit(solution)/shard_map/pkgt,pkdt->pkgd/dot_general | solution.py:75
  77.6 1.3 fusion.17
  79.0 2.0 %convolution_convert_fusion = bf16[64,1536]{1,0:T(8,128)(2,1)} fusion(bf16[64,192]{0,1:T(8,128)(2,1)S(1)} %bitcast.111, bf16[1,192,1536]{2,1,0:T(8,128)(2,1)} %param.20), kind=kOutput, calls=%fused_computation.13 | convolution fusion | flops 37847040 | bytes 811008 | tf_op jit(solution)/shard_map/dot_general | solution.py:141
  81.0 0.8 copy.97
  82.6 27.9 %reduce-scatter.2.cloned.1.call-done = bf16[8,1536]{1,0:T(8,128)(2,1)} async-done(((bf16[64,1536]{1,0:T(8,128)(2,1)}), bf16[8,1536]{1,0:T(8,128)(2,1)}) %reduce-scatter.2.cloned.1.call-update) | async-done | bytes 24592 | tf_op jit(solution)/shard_map/reduce_scatter | solution.py:140
  110.5 0.9 fusion.41
  111.5 0.9 fusion.59
  113.5 0.7 reshape.281
  114.1 6.8 %all-to-all-start = ((bf16[16,2,1,1536]{3,1,2,0:T(2,128)(2,1)}), bf16[16,2,1,1536]{3,1,2,0:T(2,128)(2,1)S(1)}, u32[]{:S(2)}, u32[]{:S(2)}) async-start(bf16[16,2,1,1536]{3,1,2,0:T(2,128)(2,1)} %bitcast.28), calls=%async_computation.1 | async-start | bytes 196608 | tf_op jit(solution)/shard_map/all_to_all | solution.py:176
  121.1 7.7 %all-to-all-done = bf16[16,2,1,1536]{3,1,2,0:T(2,128)(2,1)S(1)} async-done(((bf16[16,2,1,1536]{3,1,2,0:T(2,128)(2,1)}), bf16[16,2,1,1536]{3,1,2,0:T(2,128)(2,1)S(1)}, u32[]{:S(2)}, u32[]{:S(2)}) %all-to-all-start) | async-done | bytes 98336 | tf_op jit(solution)/shard_map/all_to_all | solution.py:176
  128.8 4.0 %fusion.8 = f32[1,32,2048]{2,1,0:T(8,128)S(1)} fusion(bf16[32,1536]{1,0:T(8,128)(2,1)S(1)} %reshape.282, bf16[1,1536,2048]{2,1,0:T(8,128)(2,1)} %param.24), kind=kOutput, calls=%fused_computation.14 | convolution fusion | flops 201326592 | bytes 6651904 | tf_op jit(solution)/shard_map/erd,edf->erf/dot_general | solution.py:98
  133.4 0.7 transpose_reshape.3
  134.1 3.5 %all-to-all-start.1 = ((bf16[16,2,1,1536]{3,1,2,0:T(2,128)(2,1)}), bf16[16,2,1,1536]{3,1,2,0:T(2,128)(2,1)S(1)}, u32[]{:S(2)}, u32[]{:S(2)}) async-start(bf16[16,2,1,1536]{3,1,2,0:T(2,128)(2,1)} %bitcast.33), calls=%async_computation.2 | async-start | bytes 196608 | tf_op jit(solution)/shard_map/all_to_all | solution.py:177
  137.7 7.6 %all-to-all-done.1 = bf16[16,2,1,1536]{3,1,2,0:T(2,128)(2,1)S(1)} async-done(((bf16[16,2,1,1536]{3,1,2,0:T(2,128)(2,1)}), bf16[16,2,1,1536]{3,1,2,0:T(2,128)(2,1)S(1)}, u32[]{:S(2)}, u32[]{:S(2)}) %all-to-all-start.1) | async-done | bytes 98336 | tf_op jit(solution)/shard_map/all_to_all | solution.py:177
  (57 shorter events, 5.4 us)
Async XLA Ops:
  6.5 126.2 %copy-start = (bf16[1,1024,1536]{2,1,0:T(8,128)(2,1)S(1)}, bf16[1,1024,1536]{2,1,0:T(8,128)(2,1)}, u32[]{:S(2)}) copy-start(bf16[1,1024,1536]{2,1,0:T(8,128)(2,1)} %param.25) | copy-start | bytes 9437188
  6.5 104.0 %reduce-scatter.2.cloned.1.call-start = ((), (), s32[]{:S(2)}) async-start(), calls=%async_computation.3 | async-start | bytes 221184 | tf_op jit(solution)/shard_map/reduce_scatter | solution.py:140
  57.5 0.9 copy-start.1
  58.4 8.0 %slice-start = ((bf16[64,1,320]{2,0,1:T(8,128)(2,1)}), bf16[64,1,192]{2,0,1:T(8,128)(2,1)S(1)}, s32[]{:S(2)}) async-start(bf16[64,1,320]{2,0,1:T(8,128)(2,1)} %copy-done.1), calls=%async_computation.4 | async-start | bytes 65536 | tf_op jit(solution)/shard_map/slice | solution.py:25
  59.4 7.0 %copy-start.3 = (f32[64,64]{1,0:T(8,128)S(1)}, f32[64,64]{1,0:T(8,128)}, u32[]{:S(2)}) copy-start(f32[64,64]{1,0:T(8,128)} %get-tuple-element.8) | copy-start | bytes 49156
  59.5 6.8 %copy-start.2 = (pred[320,128]{1,0:T(8,128)(4,1)}, pred[320,128]{1,0:T(8,128)(4,1)S(1)}, u32[]{:S(2)}) copy-start(pred[320,128]{1,0:T(8,128)(4,1)S(1)} %add_compare_fusion) | copy-start | bytes 122884
  68.7 42.6 %copy-start.4 = (f32[1536]{0:T(1024)S(1)}, f32[1536]{0:T(1024)}, u32[]{:S(2)}) copy-start(f32[1536]{0:T(1024)} %param.21) | copy-start | bytes 18436
  114.1 14.6 %all-to-all-start = ((bf16[16,2,1,1536]{3,1,2,0:T(2,128)(2,1)}), bf16[16,2,1,1536]{3,1,2,0:T(2,128)(2,1)S(1)}, u32[]{:S(2)}, u32[]{:S(2)}) async-start(bf16[16,2,1,1536]{3,1,2,0:T(2,128)(2,1)} %bitcast.28), calls=%async_computation.1 | async-start | bytes 196608 | tf_op jit(solution)/shard_map/all_to_all | solution.py:176
  134.1 11.3 %all-to-all-start.1 = ((bf16[16,2,1,1536]{3,1,2,0:T(2,128)(2,1)}), bf16[16,2,1,1536]{3,1,2,0:T(2,128)(2,1)S(1)}, u32[]{:S(2)}, u32[]{:S(2)}) async-start(bf16[16,2,1,1536]{3,1,2,0:T(2,128)(2,1)} %bitcast.33), calls=%async_computation.2 | async-start | bytes 196608 | tf_op jit(solution)/shard_map/all_to_all | solution.py:177
Sparse Core Ops, SparseCore 0:
  81.1 29.3 reduce-scatter.1
where the time goes:
time: 154 us; the launch traced here: 153 us
  waiting for transfers between devices  43.2 us (28%)
  blocking collectives  40.8 us (26%)
  matrix products  24.8 us (16%)
  between operations  13.6 us (9%)
  local copies, waits for them, and re-layouts  11.7 us (8%)
  starting transfers between devices  10.3 us (7%)
  other arithmetic  8.5 us (6%)
    reduce_scatter x1, waiting for transfers between devices, shards(): lax.psum_scatter(jnp.dot(head_out, out_flat, preferred_element_type=jnp.f...  27.9 us
    all_gather x1, blocking collectives, shards(): every_row = lax.all_gather(hidden, 'req', axis=0, tiled=True)  26.8 us
    all_gather x1, blocking collectives, shards(): tokens = lax.all_gather(picked_rows, 'kv', axis=1, tiled=True)  14 us
    all_to_all x1, waiting for transfers between devices, shards(): lax.all_to_all(outgoing, 'req', split_axis=0, concat_axis=0, tiled=True)  7.69 us
    all_to_all x1, waiting for transfers between devices, shards(): lax.all_to_all(expert_apply(arrived, gate_up, down), 'req', split_axis=0,...  7.62 us
    all_to_all x1, starting transfers between devices, shards(): lax.all_to_all(outgoing, 'req', split_axis=0, concat_axis=0, tiled=True)  6.8 us
    dot_general x1, matrix products, attend(): jnp.einsum('pkgt,pkdt->pkgd', weights.astype(jnp.bfloat16), kv_cache[:, :...  6.5 us
    dot_general x1, matrix products, attend(): jnp.einsum('pkgd,pkdt->pkgt', page_queries, kv_cache[:, :, :head_dim, :],...  5.63 us
  transfers between devices with their start and end apart: 3, of which 3 were waited for; matrix products, arithmetic and copies ran while one was open for 1% of the time, Pallas kernels for 0%

commit v1 on v0

--- a/solution.py
+++ b/solution.py
@@ -131,7 +131,12 @@
     picked_rows = jnp.dot(pick, every_row, preferred_element_type=jnp.float32).astype(
         every_row.dtype
     )
-    tokens = lax.all_gather(picked_rows, "kv", axis=1, tiled=True)
+    ring = [picked_rows]
+    for hop in range(7):
+        ring.append(lax.ppermute(ring[-1], "kv", [(dev, (dev + 1) % 8) for dev in range(8)]))
+    tokens = jnp.roll(
+        jnp.concatenate(ring[::-1], axis=1), (lax.axis_index("kv") + 1) * ring[0].shape[1], axis=1
+    )
     normed = rms_norm(tokens, attn_gain)
     head_out = attend(normed, seq_lens, page_table, kv_cache, qkv_weight)
     sub_rows = routes.shape[0]

time: 154 us -> 179 us (1.16)
  waiting for transfers between devices: 43.2 us -> 65.5 us
  blocking collectives: 40.8 us -> 27 us
  local copies, waits for them, and re-layouts: 11.7 us -> 18.2 us
  other arithmetic: 8.5 us -> 14.8 us
  matrix products: 24.8 us -> 27.6 us
    ppermute x0 -> x7, waiting for transfers between devices: none -> 24.5 us  [shards(): lax.ppermute(ring[-1], 'kv', [(dev, (dev + 1) % 8) for dev in range(8)])]
    all_gather x1 -> x0, blocking collectives: 14 us -> none  [shards(): tokens = lax.all_gather(picked_rows, 'kv', axis=1, tiled=True)]
    reduce_scatter x1, waiting for transfers between devices: 27.9 us -> 25.6 us  [shards(): lax.psum_scatter(jnp.dot(head_out, out_flat, preferred_element_type=jnp.f...]
    unnamed x15 -> x40, local copies, waits for them, and re-layouts: 3.09 us -> 5.14 us
  transfers between devices with their start and end apart: 3 -> 10, of which waited for: 3 -> 10; matrix products, arithmetic and copies ran while one was open for 1% -> 5% of each run, Pallas kernels for 0% -> 0%
where the time goes in v1:
time: 179 us; the launch traced here: 177 us
  waiting for transfers between devices  65.5 us (37%)
  matrix products  27.6 us (15%)
  blocking collectives  27 us (15%)
  local copies, waits for them, and re-layouts  18.2 us (10%)
  other arithmetic  14.8 us (8%)
  between operations  13.7 us (8%)
  starting transfers between devices  10.3 us (6%)
    all_gather x1, blocking collectives, shards(): every_row = lax.all_gather(hidden, 'req', axis=0, tiled=True)  27 us
    reduce_scatter x1, waiting for transfers between devices, shards(): lax.psum_scatter(jnp.dot(head_out, out_flat, preferred_element_type=jnp.f...  25.6 us
    ppermute x7, waiting for transfers between devices, shards(): lax.ppermute(ring[-1], 'kv', [(dev, (dev + 1) % 8) for dev in range(8)])  24.5 us
    all_to_all x1, waiting for transfers between devices, shards(): lax.all_to_all(outgoing, 'req', split_axis=0, concat_axis=0, tiled=True)  7.69 us
    all_to_all x1, waiting for transfers between devices, shards(): lax.all_to_all(expert_apply(arrived, gate_up, down), 'req', split_axis=0,...  7.62 us
    all_to_all x1, starting transfers between devices, shards(): lax.all_to_all(outgoing, 'req', split_axis=0, concat_axis=0, tiled=True)  6.8 us
    dot_general x1, matrix products, attend(): jnp.einsum('pkgt,pkdt->pkgd', weights.astype(jnp.bfloat16), kv_cache[:, :...  6.57 us
    dot_general x1, matrix products, attend(): jnp.einsum('pkgd,pkdt->pkgt', page_queries, kv_cache[:, :, :head_dim, :],...  5.62 us
  transfers between devices with their start and end apart: 10, of which 10 were waited for; matrix products, arithmetic and copies ran while one was open for 5% of the time, Pallas kernels for 0%

profile of v1, /device:TPU:0, one launch (start us, length us, event | category | flops | bytes accessed | tf_op | source)
XLA Modules:
  0.0 177.2 jit_solution(10668790227598191121)
XLA Ops:
  6.5 27.0 %all_gather.3 = bf16[1024,192]{1,0:T(8,128)(2,1)} all-gather(bf16[64,192]{1,0:T(8,128)(2,1)} %param.13), channel_id=1, replica_groups=mesh['req'=16,'kv'=8] {'req'}, dimensions={0}, use_global_device_ids=true | all-gather | bytes 417792 | tf_op jit(solution)/shard_map/all_gather | solution.py:126
  34.3 1.3 convolution_convert_fusion.3
  38.1 2.1 %collective-permute-done = bf16[64,192]{1,0:T(8,128)(2,1)S(1)} collective-permute-done((bf16[64,192]{1,0:T(8,128)(2,1)S(1)}, bf16[64,192]{1,0:T(8,128)(2,1)S(1)}, u32[]{:S(2)}, u32[]{:S(2)}) %collective-permute-start) | collective-permute-done | bytes 24608 | tf_op jit(solution)/shard_map/ppermute | solution.py:136
  40.2 0.9 fusion.7
  41.1 3.6 %collective-permute-done.1 = bf16[64,192]{1,0:T(8,128)(2,1)S(1)} collective-permute-done((bf16[64,192]{1,0:T(8,128)(2,1)S(1)}, bf16[64,192]{1,0:T(8,128)(2,1)S(1)}, u32[]{:S(2)}, u32[]{:S(2)}) %collective-permute-start.1) | collective-permute-done | bytes 24608 | tf_op jit(solution)/shard_map/ppermute | solution.py:136
  45.5 3.8 %collective-permute-done.2 = bf16[64,192]{1,0:T(8,128)(2,1)S(1)} collective-permute-done((bf16[64,192]{1,0:T(8,128)(2,1)S(1)}, bf16[64,192]{1,0:T(8,128)(2,1)S(1)}, u32[]{:S(2)}, u32[]{:S(2)}) %collective-permute-start.2) | collective-permute-done | bytes 24608 | tf_op jit(solution)/shard_map/ppermute | solution.py:136
  50.9 2.9 %collective-permute-done.3 = bf16[64,192]{1,0:T(8,128)(2,1)S(1)} collective-permute-done((bf16[64,192]{1,0:T(8,128)(2,1)S(1)}, bf16[64,192]{1,0:T(8,128)(2,1)S(1)}, u32[]{:S(2)}, u32[]{:S(2)}) %collective-permute-start.3) | collective-permute-done | bytes 24608 | tf_op jit(solution)/shard_map/ppermute | solution.py:136
  54.0 4.4 %collective-permute-done.4 = bf16[64,192]{1,0:T(8,128)(2,1)S(1)} collective-permute-done((bf16[64,192]{1,0:T(8,128)(2,1)S(1)}, bf16[64,192]{1,0:T(8,128)(2,1)S(1)}, u32[]{:S(2)}, u32[]{:S(2)}) %collective-permute-start.4) | collective-permute-done | bytes 24608 | tf_op jit(solution)/shard_map/ppermute | solution.py:136
  58.7 4.3 %collective-permute-done.5 = bf16[64,192]{1,0:T(8,128)(2,1)S(1)} collective-permute-done((bf16[64,192]{1,0:T(8,128)(2,1)S(1)}, bf16[64,192]{1,0:T(8,128)(2,1)S(1)}, u32[]{:S(2)}, u32[]{:S(2)}) %collective-permute-start.5) | collective-permute-done | bytes 24608 | tf_op jit(solution)/shard_map/ppermute | solution.py:136
  64.3 3.3 %collective-permute-done.6 = bf16[64,192]{1,0:T(8,128)(2,1)} collective-permute-done((bf16[64,192]{1,0:T(8,128)(2,1)S(1)}, bf16[64,192]{1,0:T(8,128)(2,1)}, u32[]{:S(2)}, u32[]{:S(2)}) %collective-permute-start.6) | collective-permute-done | bytes 24608 | tf_op jit(solution)/shard_map/ppermute | solution.py:136
  67.6 1.2 concatenate.6
  69.1 1.7 convolution_bitcast_fusion
  72.1 1.6 convolution_convert_fusion.2
  73.7 1.4 copy.111
  75.1 1.5 copy.110
  76.6 1.8 %copy.86 = bf16[320,3,64]{2,1,0:T(4,128)(2,1)} copy(bf16[320,3,64]{0,2,1:T(8,128)(2,1)} %bitcast.94) | data formatting | bytes 245760 | tf_op jit(solution)/shard_map/reshape.5
  78.5 5.6 %fusion.55 = (f32[320,3]{1,0:T(8,128)}, f32[320,3,128]{2,1,0:T(4,128)}) fusion(bf16[320,3,64]{2,1,0:T(4,128)(2,1)} %copy.86, bf16[320,1,128,128]{3,2,0,1:T(8,128)(2,1)} %bitcast.97, pred[320,128]{1,0:T(8,128)(4,1)} %add_compare_fusion), kind=kOutput, calls=%fused_computation.101 | convolution fusion | flops 16096320 | bytes 6106880 | tf_op jit(solution)/shard_map/pkgd,pkdt->pkgt/dot_general | solution.py:52
  84.1 1.0 copy.87
  89.1 2.0 %fusion.21 = f32[320,3]{1,0:T(8,128)S(1)} fusion(f32[320,3,128]{2,1,0:T(4,128)} %get-tuple-element.14, f32[320,3]{1,0:T(8,128)} %copy.89, pred[320,128]{1,0:T(8,128)(4,1)} %add_compare_fusion), kind=kLoop, calls=%fused_computation.33 | loop fusion | flops 367680 | bytes 540160 | tf_op jit(solution)/shard_map/reduce_sum | solution.py:74
  91.0 6.6 %fusion.2 = f32[320,3,64]{2,1,0:T(4,128)} fusion(bf16[320,1,128,128]{3,2,0,1:T(8,128)(2,1)} %bitcast.98, f32[320,3,128]{2,1,0:T(4,128)} %get-tuple-element.14, f32[320,3]{1,0:T(8,128)} %copy.89, pred[320,128]{1,0:T(8,128)(4,1)} %add_compare_fusion), kind=kOutput, calls=%fused_computation.4 | convolution fusion | flops 16097280 | bytes 6348800 | tf_op jit(solution)/shard_map/pkgt,pkdt->pkgd/dot_general | solution.py:75
  98.5 2.0 %copy.91 = f32[320,3,64]{0,2,1:T(8,128)} copy(f32[320,3,64]{2,1,0:T(4,128)} %fusion.2) | data formatting | bytes 491520 | tf_op jit(solution)/shard_map/pkgt,pkdt->pkgd/dot_general | solution.py:75
  100.5 1.9 %fusion.17 = bf16[64,3,64]{2,0,1:T(8,128)(2,1)} fusion(f32[320,3,64]{0,2,1:T(8,128)} %copy.91, pred[64,320]{1,0:T(8,128)(4,1)} %copy-done.1, f32[64,3]{0,1:T(4,128)} %convolution_add_fusion.1, f32[64,64]{1,0:T(8,128)} %get-tuple-element.7, f32[64,3]{0,1:T(4,128)S(1)} %bitcast_convert_fusion), kind=kOutput, calls=%fused_computation.24 | convolution fusion | flops 47235072 | bytes 308736 | tf_op jit(solution)/shard_map/dot_general | solution.py:85
  102.4 1.5 copy.92
  103.9 2.0 %convolution_convert_fusion = bf16[64,1536]{1,0:T(8,128)(2,1)} fusion(bf16[64,192]{0,1:T(8,128)(2,1)} %bitcast.95, bf16[1,192,1536]{2,1,0:T(8,128)(2,1)} %param.20), kind=kOutput, calls=%fused_computation.13 | convolution fusion | flops 37847040 | bytes 811008 | tf_op jit(solution)/shard_map/dot_general | solution.py:146
  107.6 25.6 %reduce-scatter.2.cloned.1.call-done = bf16[8,1536]{1,0:T(8,128)(2,1)} async-done(((bf16[64,1536]{1,0:T(8,128)(2,1)}), bf16[8,1536]{1,0:T(8,128)(2,1)}) %reduce-scatter.2.cloned.1.call-update) | async-done | bytes 24592 | tf_op jit(solution)/shard_map/reduce_scatter | solution.py:145
  133.2 0.9 fusion.40
  135.5 0.9 fusion.57
  138.2 6.8 %all-to-all-start = ((bf16[16,2,1,1536]{3,1,2,0:T(2,128)(2,1)}), bf16[16,2,1,1536]{3,1,2,0:T(2,128)(2,1)S(1)}, u32[]{:S(2)}, u32[]{:S(2)}) async-start(bf16[16,2,1,1536]{3,1,2,0:T(2,128)(2,1)} %bitcast.24), calls=%async_computation.1 | async-start | bytes 196608 | tf_op jit(solution)/shard_map/all_to_all | solution.py:181
  145.1 7.7 %all-to-all-done = bf16[16,2,1,1536]{3,1,2,0:T(2,128)(2,1)S(1)} async-done(((bf16[16,2,1,1536]{3,1,2,0:T(2,128)(2,1)}), bf16[16,2,1,1536]{3,1,2,0:T(2,128)(2,1)S(1)}, u32[]{:S(2)}, u32[]{:S(2)}) %all-to-all-start) | async-done | bytes 98336 | tf_op jit(solution)/shard_map/all_to_all | solution.py:181
  152.9 4.0 %fusion.8 = f32[1,32,2048]{2,1,0:T(8,128)S(1)} fusion(bf16[32,1536]{1,0:T(8,128)(2,1)S(1)} %reshape.282, bf16[1,1536,2048]{2,1,0:T(8,128)(2,1)} %param.24), kind=kOutput, calls=%fused_computation.14 | convolution fusion | flops 201326592 | bytes 6651904 | tf_op jit(solution)/shard_map/erd,edf->erf/dot_general | solution.py:98
  158.1 3.5 %all-to-all-start.1 = ((bf16[16,2,1,1536]{3,1,2,0:T(2,128)(2,1)}), bf16[16,2,1,1536]{3,1,2,0:T(2,128)(2,1)S(1)}, u32[]{:S(2)}, u32[]{:S(2)}) async-start(bf16[16,2,1,1536]{3,1,2,0:T(2,128)(2,1)} %bitcast.29), calls=%async_computation.2 | async-start | bytes 196608 | tf_op jit(solution)/shard_map/all_to_all | solution.py:182
  161.8 7.6 %all-to-all-done.1 = bf16[16,2,1,1536]{3,1,2,0:T(2,128)(2,1)S(1)} async-done(((bf16[16,2,1,1536]{3,1,2,0:T(2,128)(2,1)}), bf16[16,2,1,1536]{3,1,2,0:T(2,128)(2,1)S(1)}, u32[]{:S(2)}, u32[]{:S(2)}) %all-to-all-start.1) | async-done | bytes 98336 | tf_op jit(solution)/shard_map/all_to_all | solution.py:182
  (94 shorter events, 20.8 us)
Async XLA Ops:
  6.5 150.3 %copy-start = (bf16[1,1024,1536]{2,1,0:T(8,128)(2,1)S(1)}, bf16[1,1024,1536]{2,1,0:T(8,128)(2,1)}, u32[]{:S(2)}) copy-start(bf16[1,1024,1536]{2,1,0:T(8,128)(2,1)} %param.25) | copy-start | bytes 9437188
  6.5 126.7 %reduce-scatter.2.cloned.1.call-start = ((), (), s32[]{:S(2)}) async-start(), calls=%async_computation.3 | async-start | bytes 221184 | tf_op jit(solution)/shard_map/reduce_scatter | solution.py:145
  35.6 28.6 %copy-start.3 = (bf16[64,192]{1,0:T(8,128)(2,1)}, bf16[64,192]{1,0:T(8,128)(2,1)S(1)}, u32[]{:S(2)}) copy-start(bf16[64,192]{1,0:T(8,128)(2,1)S(1)} %convolution_convert_fusion.3) | copy-start | bytes 73732
  35.6 4.6 %collective-permute-start = (bf16[64,192]{1,0:T(8,128)(2,1)S(1)}, bf16[64,192]{1,0:T(8,128)(2,1)S(1)}, u32[]{:S(2)}, u32[]{:S(2)}) collective-permute-start(bf16[64,192]{1,0:T(8,128)(2,1)S(1)} %convolution_convert_fusion.3), channel_id=1, source_target_pairs={{0,1},{1,2},{2,3},{3,4},{4,5},{5,6},{6,7},{7,0},{8,9},{9,10},{10,1... | collective-permute-start | bytes 73736 | tf_op jit(solution)/shard_map/ppermute | solution.py:136
  40.2 24.0 %copy-start.6 = (bf16[64,192]{1,0:T(8,128)(2,1)}, bf16[64,192]{1,0:T(8,128)(2,1)S(1)}, u32[]{:S(2)}) copy-start(bf16[64,192]{1,0:T(8,128)(2,1)S(1)} %collective-permute-done) | copy-start | bytes 73732
  40.2 4.6 %collective-permute-start.1 = (bf16[64,192]{1,0:T(8,128)(2,1)S(1)}, bf16[64,192]{1,0:T(8,128)(2,1)S(1)}, u32[]{:S(2)}, u32[]{:S(2)}) collective-permute-start(bf16[64,192]{1,0:T(8,128)(2,1)S(1)} %collective-permute-done), channel_id=1, source_target_pairs={{0,1},{1,2},{2,3},{3,4},{4,5},{5,6},{6,7},{7,0},{8,9},{9,10},{10,1... | collective-permute-start | bytes 73736 | tf_op jit(solution)/shard_map/ppermute | solution.py:136
  41.1 3.6 %copy-start.1 = (pred[64,320]{1,0:T(8,128)(4,1)}, pred[64,320]{1,0:T(8,128)(4,1)S(1)}, u32[]{:S(2)}) copy-start(pred[64,320]{1,0:T(8,128)(4,1)S(1)} %fusion.7) | copy-start | bytes 61444
  44.8 0.8 copy-start.7
  44.8 4.6 %collective-permute-start.2 = (bf16[64,192]{1,0:T(8,128)(2,1)S(1)}, bf16[64,192]{1,0:T(8,128)(2,1)S(1)}, u32[]{:S(2)}, u32[]{:S(2)}) collective-permute-start(bf16[64,192]{1,0:T(8,128)(2,1)S(1)} %collective-permute-done.1), channel_id=1, source_target_pairs={{0,1},{1,2},{2,3},{3,4},{4,5},{5,6},{6,7},{7,0},{8,9},{9,10},{10,1... | collective-permute-start | bytes 73736 | tf_op jit(solution)/shard_map/ppermute | solution.py:136
  49.3 14.9 %copy-start.8 = (bf16[64,192]{1,0:T(8,128)(2,1)}, bf16[64,192]{1,0:T(8,128)(2,1)S(1)}, u32[]{:S(2)}) copy-start(bf16[64,192]{1,0:T(8,128)(2,1)S(1)} %collective-permute-done.2) | copy-start | bytes 73732
  49.3 4.6 %collective-permute-start.3 = (bf16[64,192]{1,0:T(8,128)(2,1)S(1)}, bf16[64,192]{1,0:T(8,128)(2,1)S(1)}, u32[]{:S(2)}, u32[]{:S(2)}) collective-permute-start(bf16[64,192]{1,0:T(8,128)(2,1)S(1)} %collective-permute-done.2), channel_id=1, source_target_pairs={{0,1},{1,2},{2,3},{3,4},{4,5},{5,6},{6,7},{7,0},{8,9},{9,10},{10,1... | collective-permute-start | bytes 73736 | tf_op jit(solution)/shard_map/ppermute | solution.py:136
  50.9 13.3 %copy-start.15 = (s32[16]{0:T(128)}, s32[16]{0:T(128)S(1)}, u32[]{:S(2)}) copy-start(s32[16]{0:T(128)S(1)} %eq.87) | copy-start | bytes 196
  53.9 10.4 %copy-start.9 = (bf16[64,192]{1,0:T(8,128)(2,1)}, bf16[64,192]{1,0:T(8,128)(2,1)S(1)}, u32[]{:S(2)}) copy-start(bf16[64,192]{1,0:T(8,128)(2,1)S(1)} %collective-permute-done.3) | copy-start | bytes 73732
  53.9 4.6 %collective-permute-start.4 = (bf16[64,192]{1,0:T(8,128)(2,1)S(1)}, bf16[64,192]{1,0:T(8,128)(2,1)S(1)}, u32[]{:S(2)}, u32[]{:S(2)}) collective-permute-start(bf16[64,192]{1,0:T(8,128)(2,1)S(1)} %collective-permute-done.3), channel_id=1, source_target_pairs={{0,1},{1,2},{2,3},{3,4},{4,5},{5,6},{6,7},{7,0},{8,9},{9,10},{10,1... | collective-permute-start | bytes 73736 | tf_op jit(solution)/shard_map/ppermute | solution.py:136
  58.4 5.8 %copy-start.10 = (bf16[64,192]{1,0:T(8,128)(2,1)}, bf16[64,192]{1,0:T(8,128)(2,1)S(1)}, u32[]{:S(2)}) copy-start(bf16[64,192]{1,0:T(8,128)(2,1)S(1)} %collective-permute-done.4) | copy-start | bytes 73732
  58.4 4.6 %collective-permute-start.5 = (bf16[64,192]{1,0:T(8,128)(2,1)S(1)}, bf16[64,192]{1,0:T(8,128)(2,1)S(1)}, u32[]{:S(2)}, u32[]{:S(2)}) collective-permute-start(bf16[64,192]{1,0:T(8,128)(2,1)S(1)} %collective-permute-done.4), channel_id=1, source_target_pairs={{0,1},{1,2},{2,3},{3,4},{4,5},{5,6},{6,7},{7,0},{8,9},{9,10},{10,1... | collective-permute-start | bytes 73736 | tf_op jit(solution)/shard_map/ppermute | solution.py:136
  58.6 5.7 %copy-start.17 = (s32[16]{0:T(128)}, s32[16]{0:T(128)S(1)}, u32[]{:S(2)}) copy-start(s32[16]{0:T(128)S(1)} %select_reduce_fusion.4) | copy-start | bytes 196
  63.0 1.3 copy-start.11
  63.0 4.7 %collective-permute-start.6 = (bf16[64,192]{1,0:T(8,128)(2,1)S(1)}, bf16[64,192]{1,0:T(8,128)(2,1)}, u32[]{:S(2)}, u32[]{:S(2)}) collective-permute-start(bf16[64,192]{1,0:T(8,128)(2,1)S(1)} %collective-permute-done.5), channel_id=1, source_target_pairs={{0,1},{1,2},{2,3},{3,4},{4,5},{5,6},{6,7},{7,0},{8,9},{9,10},{10,1... | collective-permute-start | bytes 73736 | tf_op jit(solution)/shard_map/ppermute | solution.py:136
  86.8 0.6 copy-start.12
  89.0 8.6 %copy-start.2 = (pred[64,320]{1,0:T(8,128)(4,1)S(1)}, pred[64,320]{1,0:T(8,128)(4,1)}, u32[]{:S(2)}) copy-start(pred[64,320]{1,0:T(8,128)(4,1)} %copy-done.1) | copy-start | bytes 61444
  89.0 8.6 %copy-start.13 = (f32[64,3]{0,1:T(4,128)S(1)}, f32[64,3]{0,1:T(4,128)}, u32[]{:S(2)}) copy-start(f32[64,3]{0,1:T(4,128)} %copy-done.12) | copy-start | bytes 2308
  89.0 11.4 %copy-start.16 = (bf16[64,1,3]{0,2,1:T(4,128)(2,1)S(1)}, bf16[64,1,3]{0,2,1:T(4,128)(2,1)}, u32[]{:S(2)}) copy-start(bf16[64,1,3]{0,2,1:T(4,128)(2,1)} %get-tuple-element.11) | copy-start | bytes 1156
  89.0 17.8 %copy-start.14 = (s32[8,2]{1,0:T(8,128)S(1)}, s32[8,2]{1,0:T(8,128)}, u32[]{:S(2)}) copy-start(s32[8,2]{1,0:T(8,128)} %get-tuple-element.9) | copy-start | bytes 196
  134.1 0.6 copy-start.4
  138.2 14.6 %all-to-all-start = ((bf16[16,2,1,1536]{3,1,2,0:T(2,128)(2,1)}), bf16[16,2,1,1536]{3,1,2,0:T(2,128)(2,1)S(1)}, u32[]{:S(2)}, u32[]{:S(2)}) async-start(bf16[16,2,1,1536]{3,1,2,0:T(2,128)(2,1)} %bitcast.24), calls=%async_computation.1 | async-start | bytes 196608 | tf_op jit(solution)/shard_map/all_to_all | solution.py:181
  152.9 16.8 %copy-start.5 = (bf16[8,1536]{1,0:T(8,128)(2,1)S(1)}, bf16[8,1536]{1,0:T(8,128)(2,1)}, u32[]{:S(2)}) copy-start(bf16[8,1536]{1,0:T(8,128)(2,1)} %copy-done.4) | copy-start | bytes 73732
  158.1 11.3 %all-to-all-start.1 = ((bf16[16,2,1,1536]{3,1,2,0:T(2,128)(2,1)}), bf16[16,2,1,1536]{3,1,2,0:T(2,128)(2,1)S(1)}, u32[]{:S(2)}, u32[]{:S(2)}) async-start(bf16[16,2,1,1536]{3,1,2,0:T(2,128)(2,1)} %bitcast.29), calls=%async_computation.2 | async-start | bytes 196608 | tf_op jit(solution)/shard_map/all_to_all | solution.py:182
Sparse Core Ops, SparseCore 0:
  106.1 27.0 reduce-scatter.1
